TPU v7x, 32 devices: a whole 2x2x4 slice. The times are simulated.
32 devices in a mesh: rows: 16 (over z, y, x), vecs: 2 (over core).
Axes of the slice: x: 2, y: 2, z: 4, core: 2. Of those that a mesh axis runs over, the one named last changes fastest.
Arguments:
- vectors: bfloat16 [8192, 256], P('rows', 'vecs'), may hold values from -6 to 6
- blocks: bfloat16 [64, 32, 128, 128], P('rows'), may hold values from -0.09375 to 0.09375
- scales: float32 [64, 32], P('rows'), may hold values from 0.5 to 1.5
- columns: int32 [64, 32], P('rows'), may hold values from 0 to 63, as said below
- owners: int32 [64], P('rows'), may hold values from 0 to 63, as said below
- center: float32 [1], replicated, may hold values from -0.3 to 0.3
- half_width: float32 [1], replicated, may hold values from 1.5 to 2.5
Outputs:
- filtered: bfloat16 [8192, 256], P('rows', 'vecs')
Inputs may be any that keep to these rules, and one draw needn't show every extreme that they name: `columns`: the block rows of one aligned group of 4 block rows read at most one atom of each aligned group of 4 atoms. owners is a permutation of the atoms; the 4 entries of one aligned group of 4 entries lie in distinct aligned groups of 4 atoms.
All inputs are finite; a program needn't handle non-finite values.
Results may differ from a plain program's by a relative error of at most 0.0054.
Values may be sent and summed in bfloat16 or wider, within the bound.
No kernel may reach another device: no remote copies, remote signals or barrier semaphores. Data moves between devices by JAX's collectives and lax.ppermute only.
A program may use at most 64 MiB of HBM per device.

v0:
```python
import jax
import jax.numpy as jnp
from jax import lax
from jax.sharding import PartitionSpec as P

STEPS = 4


def on_device(vectors, blocks, scales, columns, owners, center, half_width):
    local_rows = blocks.shape[0]
    per_row = blocks.shape[1]
    orbitals = blocks.shape[2]
    group_width = vectors.shape[1]

    def gather_all(panels):
        return lax.all_gather(panels, "rows", axis=0, tiled=True)

    def apply_blocks(panels):
        everything = gather_all(panels)
        operand = jnp.take(everything, columns.reshape(-1), axis=0).reshape(
            local_rows, per_row, orbitals, group_width
        )
        partial_value = jnp.einsum(
            "rkij,rkjv->rkiv", blocks, operand, preferred_element_type=jnp.float32
        )
        return jnp.sum(partial_value * scales[:, :, None, None], axis=1)

    shift = center[0]
    width = half_width[0]
    previous = vectors.reshape(local_rows, orbitals, group_width)
    current = ((apply_blocks(previous) - shift * previous.astype(jnp.float32)) / width).astype(
        jnp.bfloat16
    )
    for step in range(STEPS - 1):
        image = apply_blocks(current)
        upcoming = (
            2.0 * (image - shift * current.astype(jnp.float32)) / width
            - previous.astype(jnp.float32)
        ).astype(jnp.bfloat16)
        previous, current = (current, upcoming)
    placed = jnp.take(gather_all(current), owners, axis=0)
    return placed.reshape(local_rows * orbitals, group_width)


def solution(mesh):
    in_specs = (
        P("rows", "vecs"),
        P("rows", None, None, None),
        P("rows", None),
        P("rows", None),
        P("rows"),
        P(),
        P(),
    )
    out_specs = P("rows", "vecs")
    return jax.shard_map(
        on_device, mesh=mesh, in_specs=in_specs, out_specs=out_specs, check_vma=False
    )
```

profile of v0, /device:TPU:0, one launch (start us, length us, event | category | flops | bytes accessed | tf_op | source)
XLA Modules:
  0.0 369.5 jit_solution(10198902864211018663)
XLA Ops:
  6.5 0.0 all-gather.6.cloned.1.call-start
  6.5 0.7 all-gather.6.cloned.1.call-update
  7.3 0.0 all-gather.8.cloned.1.call-start
  7.3 1.0 copy.22
  8.3 0.8 reshape.36
  10.4 63.1 %all-gather.6.cloned.1.call-done = bf16[64,128,128]{2,1,0:T(8,128)(2,1)} async-done(((bf16[4,128,128]{2,1,0:T(8,128)(2,1)}), bf16[64,128,128]{2,1,0:T(8,128)(2,1)}) %all-gather.6.cloned.1.call-update) | async-done | bytes 2097168 | tf_op jit(solution)/shard_map/all_gather | solution.py:16
  73.6 4.6 %gather_fusion.1 = bf16[128,128,128]{2,1,0:T(8,128)(2,1)} fusion(bf16[64,128,128]{2,1,0:T(8,128)(2,1)} %all-gather.6.cloned.1.call-done, s32[1024]{0:T(1024)S(1)} %pad_clamp_fusion.1), kind=kCustom, calls=%fused_computation.clone | custom fusion | bytes 8389120 | tf_op jit(solution)/shard_map/jit(_take)/gather | solution.py:20
  78.2 0.0 copy-start
  78.2 0.0 copy-start.4
  78.2 2.8 broadcast_select_fusion
  81.0 0.7 copy-done
  81.6 0.0 copy-done.4
  81.6 3.2 multiply_reduce_fusion.3
  84.8 0.1 fusion.2
  84.8 0.8 copy.23
  85.6 0.0 all-gather.8.cloned.1.call-update
  85.6 0.0 all-gather.10.cloned.1.call-start
  85.7 59.5 %all-gather.8.cloned.1.call-done = bf16[64,128,128]{2,1,0:T(8,128)(2,1)} async-done(((bf16[4,128,128]{2,1,0:T(8,128)(2,1)}), bf16[64,128,128]{2,1,0:T(8,128)(2,1)}) %all-gather.8.cloned.1.call-update) | async-done | bytes 2097168 | tf_op jit(solution)/shard_map/all_gather | solution.py:16
  145.2 4.6 %gather_fusion.2 = bf16[128,128,128]{2,1,0:T(8,128)(2,1)} fusion(bf16[64,128,128]{2,1,0:T(8,128)(2,1)} %all-gather.8.cloned.1.call-done, s32[1024]{0:T(1024)S(1)} %pad_clamp_fusion.1), kind=kCustom, calls=%fused_computation.1.clone | custom fusion | bytes 8389120 | tf_op jit(solution)/shard_map/jit(_take)/gather | solution.py:20
  149.8 2.8 broadcast_select_fusion.1
  152.6 0.7 copy-done.1
  153.2 3.1 multiply_reduce_fusion.2
  156.4 0.1 fusion.3
  156.5 0.8 copy.25
  157.2 0.0 all-gather.10.cloned.1.call-update
  157.3 0.0 all-gather.12.cloned.1.call-start
  157.3 59.5 %all-gather.10.cloned.1.call-done = bf16[64,128,128]{2,1,0:T(8,128)(2,1)} async-done(((bf16[4,128,128]{2,1,0:T(8,128)(2,1)}), bf16[64,128,128]{2,1,0:T(8,128)(2,1)}) %all-gather.10.cloned.1.call-update) | async-done | bytes 2097168 | tf_op jit(solution)/shard_map/all_gather | solution.py:16
  216.8 4.6 %gather_fusion.3 = bf16[128,128,128]{2,1,0:T(8,128)(2,1)} fusion(bf16[64,128,128]{2,1,0:T(8,128)(2,1)} %all-gather.10.cloned.1.call-done, s32[1024]{0:T(1024)S(1)} %pad_clamp_fusion.1), kind=kCustom, calls=%fused_computation.2.clone | custom fusion | bytes 8389120 | tf_op jit(solution)/shard_map/jit(_take)/gather | solution.py:20
  221.4 2.8 broadcast_select_fusion.2
  224.2 0.7 copy-done.2
  224.8 3.1 multiply_reduce_fusion.1
  228.0 0.1 fusion.7
  228.1 0.8 copy.27
  228.8 0.0 all-gather.12.cloned.1.call-update
  228.9 0.2 all-gather.14.cloned.1.call-start
  229.1 59.3 %all-gather.12.cloned.1.call-done = bf16[64,128,128]{2,1,0:T(8,128)(2,1)} async-done(((bf16[4,128,128]{2,1,0:T(8,128)(2,1)}), bf16[64,128,128]{2,1,0:T(8,128)(2,1)}) %all-gather.12.cloned.1.call-update) | async-done | bytes 2097168 | tf_op jit(solution)/shard_map/all_gather | solution.py:16
  288.4 4.6 %gather_fusion.4 = bf16[128,128,128]{2,1,0:T(8,128)(2,1)} fusion(bf16[64,128,128]{2,1,0:T(8,128)(2,1)} %all-gather.12.cloned.1.call-done, s32[1024]{0:T(1024)S(1)} %pad_clamp_fusion.1), kind=kCustom, calls=%fused_computation.3.clone | custom fusion | bytes 8389120 | tf_op jit(solution)/shard_map/jit(_take)/gather | solution.py:20
  293.0 2.8 broadcast_select_fusion.3
  295.8 0.7 copy-done.3
  296.4 3.1 multiply_reduce_fusion
  299.6 0.1 fusion.11
  299.7 0.8 copy.29
  300.5 0.0 all-gather.14.cloned.1.call-update
  300.5 0.0 copy-done.5
  300.5 0.1 broadcast_bitcast_fusion
  300.6 59.4 %all-gather.14.cloned.1.call-done = bf16[64,128,128]{2,1,0:T(8,128)(2,1)} async-done(((bf16[4,128,128]{2,1,0:T(8,128)(2,1)}), bf16[64,128,128]{2,1,0:T(8,128)(2,1)}) %all-gather.14.cloned.1.call-update) | async-done | bytes 2097168 | tf_op jit(solution)/shard_map/all_gather | solution.py:16
  360.0 2.2 gather_fusion
  362.2 0.8 bitcast_select_fusion
  (10 shorter events, 0.0 us)
Async XLA Ops:
  6.5 67.0 %all-gather.6.cloned.1.call-start = ((), (), s32[]{:S(2)}) async-start(), calls=%async_computation | async-start | bytes 2228224 | tf_op jit(solution)/shard_map/all_gather | solution.py:16
  7.3 137.9 %all-gather.8.cloned.1.call-start = ((), (), s32[]{:S(2)}) async-start(), calls=%async_computation.1 | async-start | bytes 2228224 | tf_op jit(solution)/shard_map/all_gather | solution.py:16
  78.2 3.4 copy-start
  78.2 3.4 copy-start.4
  85.6 131.1 %all-gather.10.cloned.1.call-start = ((), (), s32[]{:S(2)}) async-start(), calls=%async_computation.2 | async-start | bytes 2228224 | tf_op jit(solution)/shard_map/all_gather | solution.py:16
  149.8 3.4 copy-start.1
  157.3 131.1 %all-gather.12.cloned.1.call-start = ((), (), s32[]{:S(2)}) async-start(), calls=%async_computation.3 | async-start | bytes 2228224 | tf_op jit(solution)/shard_map/all_gather | solution.py:16
  221.4 3.4 copy-start.2
  228.9 131.1 %all-gather.14.cloned.1.call-start = ((), (), s32[]{:S(2)}) async-start(), calls=%async_computation.4 | async-start | bytes 2228224 | tf_op jit(solution)/shard_map/all_gather | solution.py:16
  293.0 3.4 copy-start.3
  296.4 4.0 %copy-start.5 = (s32[4]{0:T(128)S(1)}, s32[4]{0:T(128)}, u32[]{:S(2)}) copy-start(s32[4]{0:T(128)} %param.13) | copy-start | bytes 52
Sparse Core Ops, SparseCore 0:
  10.1 63.3 all-gather.5
  85.8 59.3 all-gather.7
  157.4 59.3 all-gather.9
  229.0 59.3 all-gather.11
  300.6 59.3 all-gather.13
where the time goes:
time: 370 us; the launch traced here: 369 us
  waiting for transfers between devices  301 us (81%)
  local copies, waits for them, and re-layouts  28.2 us (8%)
  between operations  14.6 us (4%)
  matrix products  12.6 us (3%)
  other arithmetic  12.2 us (3%)
    all_gather x5, waiting for transfers between devices, gather_all(): return lax.all_gather(panels, 'rows', axis=0, tiled=True)  301 us
    gather x4, local copies, waits for them, and re-layouts, apply_blocks(): jnp.take(everything, columns.reshape(-1), axis=0)  18.5 us
    dot_general x4, matrix products, apply_blocks(): jnp.einsum('rkij,rkjv->rkiv', blocks, operand, preferred_element_type=jnp...  12.6 us
    select_n x5, other arithmetic, apply_blocks(): jnp.take(everything, columns.reshape(-1), axis=0)  11.1 us
  transfers between devices with their start and end apart: 5, of which 5 were waited for; matrix products, arithmetic and copies ran while one was open for 1% of the time, Pallas kernels for 0%

commit v1 on v0

--- a/solution.py
+++ b/solution.py
@@ -4,6 +4,19 @@
 from jax.sharding import PartitionSpec as P
 
 STEPS = 4
+
+
+def collect(value, axis, dim):
+    ways = lax.axis_size(axis)
+    up = [(d, (d + 1) % ways) for d in range(ways)]
+    down = [(d, (d - 1) % ways) for d in range(ways)]
+    earlier, later = ([value], [value])
+    for _ in range(ways // 2):
+        earlier.append(lax.ppermute(earlier[-1], axis, up))
+    for _ in range((ways - 1) // 2):
+        later.append(lax.ppermute(later[-1], axis, down))
+    line = jnp.concatenate([*earlier[::-1], *later[1:]], axis=dim)
+    return jnp.roll(line, (lax.axis_index(axis) - ways // 2) * value.shape[dim], axis=dim)
 
 
 def on_device(vectors, blocks, scales, columns, owners, center, half_width):
@@ -13,7 +26,7 @@
     group_width = vectors.shape[1]
 
     def gather_all(panels):
-        return lax.all_gather(panels, "rows", axis=0, tiled=True)
+        return collect(panels, "rows", 0)
 
     def apply_blocks(panels):
         everything = gather_all(panels)

time: 370 us -> 407 us (1.10)
  starting transfers between devices: 0.35 us -> 202 us
  waiting for transfers between devices: 301 us -> 155 us
  between operations: 14.6 us -> 2.23 us
  local copies, waits for them, and re-layouts: 28.2 us -> 19.1 us
    all_gather x5 -> x0, waiting for transfers between devices: 301 us -> none  [gather_all(): return lax.all_gather(panels, 'rows', axis=0, tiled=True)]
    ppermute x0 -> x75, starting transfers between devices: none -> 202 us  [the longest x35 199 us: collect(): later.append(lax.ppermute(later[-1], axis, down))]
    ppermute x0 -> x75, waiting for transfers between devices: none -> 155 us  [the longest x40 153 us: collect(): earlier.append(lax.ppermute(earlier[-1], axis, up))]
    gather x4, local copies, waits for them, and re-layouts: 18.5 us -> 12.3 us  [apply_blocks(): jnp.take(everything, columns.reshape(-1), axis=0)]
  transfers between devices with their start and end apart: 5 -> 75, of which waited for: 5 -> 42; matrix products, arithmetic and copies ran while one was open for 1% -> 1% of each run, Pallas kernels for 0% -> 0%
where the time goes in v1:
time: 407 us
  starting transfers between devices  202 us (50%)
  waiting for transfers between devices  155 us (38%)
  local copies, waits for them, and re-layouts  19.1 us (5%)
  other arithmetic  16.2 us (4%)
  matrix products  12.2 us (3%)
    ppermute x35, starting transfers between devices, collect(): later.append(lax.ppermute(later[-1], axis, down))  199 us
    ppermute x40, waiting for transfers between devices, collect(): earlier.append(lax.ppermute(earlier[-1], axis, up))  153 us
    gather x4, local copies, waits for them, and re-layouts, apply_blocks(): jnp.take(everything, columns.reshape(-1), axis=0)  12.3 us
    dot_general x4, matrix products, apply_blocks(): jnp.einsum('rkij,rkjv->rkiv', blocks, operand, preferred_element_type=jnp...  12.2 us
    select_n x5, other arithmetic, apply_blocks(): jnp.take(everything, columns.reshape(-1), axis=0)  11.1 us
  transfers between devices with their start and end apart: 75, of which 42 were waited for; matrix products, arithmetic and copies ran while one was open for 1% of the time, Pallas kernels for 0%

profile of v1, /device:TPU:0, one launch (start us, length us, event | category | flops | bytes accessed | tf_op | source)
XLA Modules:
  0.0 406.6 jit_solution(13467000095377053787)
XLA Ops:
  2.9 7.8 %collective-permute-done = bf16[4,128,128]{2,1,0:T(8,128)(2,1)S(1)} collective-permute-done((bf16[4,128,128]{2,1,0:T(8,128)(2,1)}, bf16[4,128,128]{2,1,0:T(8,128)(2,1)S(1)}, u32[]{:S(2)}, u32[]{:S(2)}) %collective-permute-start) | collective-permute-done | bytes 131104 | tf_op jit(solution)/shard_map/ppermute | solution.py:15
  10.7 5.6 %collective-permute-start.8 = (bf16[4,128,128]{2,1,0:T(8,128)(2,1)}, bf16[4,128,128]{2,1,0:T(8,128)(2,1)S(1)}, u32[]{:S(2)}, u32[]{:S(2)}) collective-permute-start(bf16[4,128,128]{2,1,0:T(8,128)(2,1)} %bitcast.46), channel_id=1, source_target_pairs={{0,30},{2,0},{4,2},{6,4},{8,6},{10,8},{12,10},{14,12},{16,14},{18,... | collective-permute-start | bytes 393224 | tf_op jit(solution)/shard_map/ppermute | solution.py:17
  19.4 5.8 %collective-permute-start.9 = (bf16[4,128,128]{2,1,0:T(8,128)(2,1)S(1)}, bf16[4,128,128]{2,1,0:T(8,128)(2,1)S(1)}, u32[]{:S(2)}, u32[]{:S(2)}) collective-permute-start(bf16[4,128,128]{2,1,0:T(8,128)(2,1)S(1)} %collective-permute-done.8), channel_id=1, source_target_pairs={{0,30},{2,0},{4,2},{6,4},{8,6},{10,8},{12,10},{14,12},{16,14},{18,... | collective-permute-start | bytes 393224 | tf_op jit(solution)/shard_map/ppermute | solution.py:17
  27.9 5.9 %collective-permute-start.10 = (bf16[4,128,128]{2,1,0:T(8,128)(2,1)S(1)}, bf16[4,128,128]{2,1,0:T(8,128)(2,1)S(1)}, u32[]{:S(2)}, u32[]{:S(2)}) collective-permute-start(bf16[4,128,128]{2,1,0:T(8,128)(2,1)S(1)} %collective-permute-done.9), channel_id=1, source_target_pairs={{0,30},{2,0},{4,2},{6,4},{8,6},{10,8},{12,10},{14,12},{16,14},{18,... | collective-permute-start | bytes 393224 | tf_op jit(solution)/shard_map/ppermute | solution.py:17
  36.6 5.8 %collective-permute-start.11 = (bf16[4,128,128]{2,1,0:T(8,128)(2,1)S(1)}, bf16[4,128,128]{2,1,0:T(8,128)(2,1)S(1)}, u32[]{:S(2)}, u32[]{:S(2)}) collective-permute-start(bf16[4,128,128]{2,1,0:T(8,128)(2,1)S(1)} %collective-permute-done.10), channel_id=1, source_target_pairs={{0,30},{2,0},{4,2},{6,4},{8,6},{10,8},{12,10},{14,12},{16,14},{18,... | collective-permute-start | bytes 393224 | tf_op jit(solution)/shard_map/ppermute | solution.py:17
  46.1 5.6 %collective-permute-start.12 = (bf16[4,128,128]{2,1,0:T(8,128)(2,1)S(1)}, bf16[4,128,128]{2,1,0:T(8,128)(2,1)S(1)}, u32[]{:S(2)}, u32[]{:S(2)}) collective-permute-start(bf16[4,128,128]{2,1,0:T(8,128)(2,1)S(1)} %collective-permute-done.11), channel_id=1, source_target_pairs={{0,30},{2,0},{4,2},{6,4},{8,6},{10,8},{12,10},{14,12},{16,14},{18,... | collective-permute-start | bytes 393224 | tf_op jit(solution)/shard_map/ppermute | solution.py:17
  54.7 6.2 %collective-permute-start.13 = (bf16[4,128,128]{2,1,0:T(8,128)(2,1)S(1)}, bf16[4,128,128]{2,1,0:T(8,128)(2,1)S(1)}, u32[]{:S(2)}, u32[]{:S(2)}) collective-permute-start(bf16[4,128,128]{2,1,0:T(8,128)(2,1)S(1)} %collective-permute-done.12), channel_id=1, source_target_pairs={{0,30},{2,0},{4,2},{6,4},{8,6},{10,8},{12,10},{14,12},{16,14},{18,... | collective-permute-start | bytes 393224 | tf_op jit(solution)/shard_map/ppermute | solution.py:17
  66.7 5.6 %collective-permute-start.14 = (bf16[4,128,128]{2,1,0:T(8,128)(2,1)S(1)}, bf16[4,128,128]{2,1,0:T(8,128)(2,1)S(1)}, u32[]{:S(2)}, u32[]{:S(2)}) collective-permute-start(bf16[4,128,128]{2,1,0:T(8,128)(2,1)S(1)} %collective-permute-done.13), channel_id=1, source_target_pairs={{0,30},{2,0},{4,2},{6,4},{8,6},{10,8},{12,10},{14,12},{16,14},{18,... | collective-permute-start | bytes 393224 | tf_op jit(solution)/shard_map/ppermute | solution.py:17
  85.5 9.0 %collective-permute-done.15 = bf16[4,128,128]{1,2,0:T(8,128)(2,1)S(1)} collective-permute-done((bf16[4,128,128]{1,2,0:T(8,128)(2,1)S(1)}, bf16[4,128,128]{1,2,0:T(8,128)(2,1)S(1)}, u32[]{:S(2)}, u32[]{:S(2)}) %collective-permute-start.15) | collective-permute-done | bytes 131104 | tf_op jit(solution)/shard_map/ppermute | solution.py:15
  94.4 5.6 %collective-permute-start.23 = (bf16[4,128,128]{1,2,0:T(8,128)(2,1)S(1)}, bf16[4,128,128]{1,2,0:T(8,128)(2,1)S(1)}, u32[]{:S(2)}, u32[]{:S(2)}) collective-permute-start(bf16[4,128,128]{1,2,0:T(8,128)(2,1)S(1)} %fusion.7), channel_id=1, source_target_pairs={{0,30},{2,0},{4,2},{6,4},{8,6},{10,8},{12,10},{14,12},{16,14},{18,... | collective-permute-start | bytes 393224 | tf_op jit(solution)/shard_map/ppermute | solution.py:17
  103.1 5.6 %collective-permute-start.24 = (bf16[4,128,128]{1,2,0:T(8,128)(2,1)S(1)}, bf16[4,128,128]{1,2,0:T(8,128)(2,1)S(1)}, u32[]{:S(2)}, u32[]{:S(2)}) collective-permute-start(bf16[4,128,128]{1,2,0:T(8,128)(2,1)S(1)} %collective-permute-done.23), channel_id=1, source_target_pairs={{0,30},{2,0},{4,2},{6,4},{8,6},{10,8},{12,10},{14,12},{16,14},{18,... | collective-permute-start | bytes 393224 | tf_op jit(solution)/shard_map/ppermute | solution.py:17
  111.8 5.6 %collective-permute-start.25 = (bf16[4,128,128]{1,2,0:T(8,128)(2,1)S(1)}, bf16[4,128,128]{1,2,0:T(8,128)(2,1)S(1)}, u32[]{:S(2)}, u32[]{:S(2)}) collective-permute-start(bf16[4,128,128]{1,2,0:T(8,128)(2,1)S(1)} %collective-permute-done.24), channel_id=1, source_target_pairs={{0,30},{2,0},{4,2},{6,4},{8,6},{10,8},{12,10},{14,12},{16,14},{18,... | collective-permute-start | bytes 393224 | tf_op jit(solution)/shard_map/ppermute | solution.py:17
  117.4 4.1 collective-permute-done.18
  121.5 5.7 %collective-permute-start.26 = (bf16[4,128,128]{1,2,0:T(8,128)(2,1)S(1)}, bf16[4,128,128]{1,2,0:T(8,128)(2,1)S(1)}, u32[]{:S(2)}, u32[]{:S(2)}) collective-permute-start(bf16[4,128,128]{1,2,0:T(8,128)(2,1)S(1)} %collective-permute-done.25), channel_id=1, source_target_pairs={{0,30},{2,0},{4,2},{6,4},{8,6},{10,8},{12,10},{14,12},{16,14},{18,... | collective-permute-start | bytes 393224 | tf_op jit(solution)/shard_map/ppermute | solution.py:17
  127.2 3.6 collective-permute-done.19
  130.8 5.6 %collective-permute-start.27 = (bf16[4,128,128]{1,2,0:T(8,128)(2,1)S(1)}, bf16[4,128,128]{1,2,0:T(8,128)(2,1)S(1)}, u32[]{:S(2)}, u32[]{:S(2)}) collective-permute-start(bf16[4,128,128]{1,2,0:T(8,128)(2,1)S(1)} %collective-permute-done.26), channel_id=1, source_target_pairs={{0,30},{2,0},{4,2},{6,4},{8,6},{10,8},{12,10},{14,12},{16,14},{18,... | collective-permute-start | bytes 393224 | tf_op jit(solution)/shard_map/ppermute | solution.py:17
  139.4 5.6 %collective-permute-start.28 = (bf16[4,128,128]{1,2,0:T(8,128)(2,1)S(1)}, bf16[4,128,128]{1,2,0:T(8,128)(2,1)S(1)}, u32[]{:S(2)}, u32[]{:S(2)}) collective-permute-start(bf16[4,128,128]{1,2,0:T(8,128)(2,1)S(1)} %collective-permute-done.27), channel_id=1, source_target_pairs={{0,30},{2,0},{4,2},{6,4},{8,6},{10,8},{12,10},{14,12},{16,14},{18,... | collective-permute-start | bytes 393224 | tf_op jit(solution)/shard_map/ppermute | solution.py:17
  148.0 5.6 %collective-permute-start.29 = (bf16[4,128,128]{1,2,0:T(8,128)(2,1)S(1)}, bf16[4,128,128]{1,2,0:T(8,128)(2,1)S(1)}, u32[]{:S(2)}, u32[]{:S(2)}) collective-permute-start(bf16[4,128,128]{1,2,0:T(8,128)(2,1)S(1)} %collective-permute-done.28), channel_id=1, source_target_pairs={{0,30},{2,0},{4,2},{6,4},{8,6},{10,8},{12,10},{14,12},{16,14},{18,... | collective-permute-start | bytes 393224 | tf_op jit(solution)/shard_map/ppermute | solution.py:17
  153.6 3.8 collective-permute-done.22
  168.3 8.7 %collective-permute-done.30 = bf16[4,128,128]{1,2,0:T(8,128)(2,1)S(1)} collective-permute-done((bf16[4,128,128]{1,2,0:T(8,128)(2,1)S(1)}, bf16[4,128,128]{1,2,0:T(8,128)(2,1)S(1)}, u32[]{:S(2)}, u32[]{:S(2)}) %collective-permute-start.30) | collective-permute-done | bytes 131104 | tf_op jit(solution)/shard_map/ppermute | solution.py:15
  177.0 5.6 %collective-permute-start.38 = (bf16[4,128,128]{1,2,0:T(8,128)(2,1)S(1)}, bf16[4,128,128]{1,2,0:T(8,128)(2,1)S(1)}, u32[]{:S(2)}, u32[]{:S(2)}) collective-permute-start(bf16[4,128,128]{1,2,0:T(8,128)(2,1)S(1)} %fusion.8), channel_id=1, source_target_pairs={{0,30},{2,0},{4,2},{6,4},{8,6},{10,8},{12,10},{14,12},{16,14},{18,... | collective-permute-start | bytes 393224 | tf_op jit(solution)/shard_map/ppermute | solution.py:17
  185.7 5.6 %collective-permute-start.39 = (bf16[4,128,128]{1,2,0:T(8,128)(2,1)S(1)}, bf16[4,128,128]{1,2,0:T(8,128)(2,1)S(1)}, u32[]{:S(2)}, u32[]{:S(2)}) collective-permute-start(bf16[4,128,128]{1,2,0:T(8,128)(2,1)S(1)} %collective-permute-done.38), channel_id=1, source_target_pairs={{0,30},{2,0},{4,2},{6,4},{8,6},{10,8},{12,10},{14,12},{16,14},{18,... | collective-permute-start | bytes 393224 | tf_op jit(solution)/shard_map/ppermute | solution.py:17
  191.3 4.2 %collective-permute-done.32 = bf16[4,128,128]{1,2,0:T(8,128)(2,1)S(1)} collective-permute-done((bf16[4,128,128]{1,2,0:T(8,128)(2,1)S(1)}, bf16[4,128,128]{1,2,0:T(8,128)(2,1)S(1)}, u32[]{:S(2)}, u32[]{:S(2)}) %collective-permute-start.32) | collective-permute-done | bytes 131104 | tf_op jit(solution)/shard_map/ppermute | solution.py:15
  195.5 5.6 %collective-permute-start.40 = (bf16[4,128,128]{1,2,0:T(8,128)(2,1)S(1)}, bf16[4,128,128]{1,2,0:T(8,128)(2,1)S(1)}, u32[]{:S(2)}, u32[]{:S(2)}) collective-permute-start(bf16[4,128,128]{1,2,0:T(8,128)(2,1)S(1)} %collective-permute-done.39), channel_id=1, source_target_pairs={{0,30},{2,0},{4,2},{6,4},{8,6},{10,8},{12,10},{14,12},{16,14},{18,... | collective-permute-start | bytes 393224 | tf_op jit(solution)/shard_map/ppermute | solution.py:17
  201.1 3.6 collective-permute-done.33
  204.7 5.6 %collective-permute-start.41 = (bf16[4,128,128]{1,2,0:T(8,128)(2,1)S(1)}, bf16[4,128,128]{1,2,0:T(8,128)(2,1)S(1)}, u32[]{:S(2)}, u32[]{:S(2)}) collective-permute-start(bf16[4,128,128]{1,2,0:T(8,128)(2,1)S(1)} %collective-permute-done.40), channel_id=1, source_target_pairs={{0,30},{2,0},{4,2},{6,4},{8,6},{10,8},{12,10},{14,12},{16,14},{18,... | collective-permute-start | bytes 393224 | tf_op jit(solution)/shard_map/ppermute | solution.py:17
  213.3 5.6 %collective-permute-start.42 = (bf16[4,128,128]{1,2,0:T(8,128)(2,1)S(1)}, bf16[4,128,128]{1,2,0:T(8,128)(2,1)S(1)}, u32[]{:S(2)}, u32[]{:S(2)}) collective-permute-start(bf16[4,128,128]{1,2,0:T(8,128)(2,1)S(1)} %collective-permute-done.41), channel_id=1, source_target_pairs={{0,30},{2,0},{4,2},{6,4},{8,6},{10,8},{12,10},{14,12},{16,14},{18,... | collective-permute-start | bytes 393224 | tf_op jit(solution)/shard_map/ppermute | solution.py:17
  221.9 5.7 %collective-permute-start.43 = (bf16[4,128,128]{1,2,0:T(8,128)(2,1)S(1)}, bf16[4,128,128]{1,2,0:T(8,128)(2,1)S(1)}, u32[]{:S(2)}, u32[]{:S(2)}) collective-permute-start(bf16[4,128,128]{1,2,0:T(8,128)(2,1)S(1)} %collective-permute-done.42), channel_id=1, source_target_pairs={{0,30},{2,0},{4,2},{6,4},{8,6},{10,8},{12,10},{14,12},{16,14},{18,... | collective-permute-start | bytes 393224 | tf_op jit(solution)/shard_map/ppermute | solution.py:17
  227.6 3.6 collective-permute-done.36
  231.3 5.6 %collective-permute-start.44 = (bf16[4,128,128]{1,2,0:T(8,128)(2,1)S(1)}, bf16[4,128,128]{1,2,0:T(8,128)(2,1)S(1)}, u32[]{:S(2)}, u32[]{:S(2)}) collective-permute-start(bf16[4,128,128]{1,2,0:T(8,128)(2,1)S(1)} %collective-permute-done.43), channel_id=1, source_target_pairs={{0,30},{2,0},{4,2},{6,4},{8,6},{10,8},{12,10},{14,12},{16,14},{18,... | collective-permute-start | bytes 393224 | tf_op jit(solution)/shard_map/ppermute | solution.py:17
  250.8 8.8 %collective-permute-done.45 = bf16[4,128,128]{1,2,0:T(8,128)(2,1)S(1)} collective-permute-done((bf16[4,128,128]{1,2,0:T(8,128)(2,1)S(1)}, bf16[4,128,128]{1,2,0:T(8,128)(2,1)S(1)}, u32[]{:S(2)}, u32[]{:S(2)}) %collective-permute-start.45) | collective-permute-done | bytes 131104 | tf_op jit(solution)/shard_map/ppermute | solution.py:15
  259.6 5.6 %collective-permute-start.53 = (bf16[4,128,128]{1,2,0:T(8,128)(2,1)S(1)}, bf16[4,128,128]{1,2,0:T(8,128)(2,1)S(1)}, u32[]{:S(2)}, u32[]{:S(2)}) collective-permute-start(bf16[4,128,128]{1,2,0:T(8,128)(2,1)S(1)} %fusion.12), channel_id=1, source_target_pairs={{0,30},{2,0},{4,2},{6,4},{8,6},{10,8},{12,10},{14,12},{16,14},{18,... | collective-permute-start | bytes 393224 | tf_op jit(solution)/shard_map/ppermute | solution.py:17
  265.2 4.3 %collective-permute-done.46 = bf16[4,128,128]{1,2,0:T(8,128)(2,1)S(1)} collective-permute-done((bf16[4,128,128]{1,2,0:T(8,128)(2,1)S(1)}, bf16[4,128,128]{1,2,0:T(8,128)(2,1)S(1)}, u32[]{:S(2)}, u32[]{:S(2)}) %collective-permute-start.46) | collective-permute-done | bytes 131104 | tf_op jit(solution)/shard_map/ppermute | solution.py:15
  269.5 5.6 %collective-permute-start.54 = (bf16[4,128,128]{1,2,0:T(8,128)(2,1)S(1)}, bf16[4,128,128]{1,2,0:T(8,128)(2,1)S(1)}, u32[]{:S(2)}, u32[]{:S(2)}) collective-permute-start(bf16[4,128,128]{1,2,0:T(8,128)(2,1)S(1)} %collective-permute-done.53), channel_id=1, source_target_pairs={{0,30},{2,0},{4,2},{6,4},{8,6},{10,8},{12,10},{14,12},{16,14},{18,... | collective-permute-start | bytes 393224 | tf_op jit(solution)/shard_map/ppermute | solution.py:17
  278.6 5.6 %collective-permute-start.55 = (bf16[4,128,128]{1,2,0:T(8,128)(2,1)S(1)}, bf16[4,128,128]{1,2,0:T(8,128)(2,1)S(1)}, u32[]{:S(2)}, u32[]{:S(2)}) collective-permute-start(bf16[4,128,128]{1,2,0:T(8,128)(2,1)S(1)} %collective-permute-done.54), channel_id=1, source_target_pairs={{0,30},{2,0},{4,2},{6,4},{8,6},{10,8},{12,10},{14,12},{16,14},{18,... | collective-permute-start | bytes 393224 | tf_op jit(solution)/shard_map/ppermute | solution.py:17
  287.3 5.6 %collective-permute-start.56 = (bf16[4,128,128]{1,2,0:T(8,128)(2,1)S(1)}, bf16[4,128,128]{1,2,0:T(8,128)(2,1)S(1)}, u32[]{:S(2)}, u32[]{:S(2)}) collective-permute-start(bf16[4,128,128]{1,2,0:T(8,128)(2,1)S(1)} %collective-permute-done.55), channel_id=1, source_target_pairs={{0,30},{2,0},{4,2},{6,4},{8,6},{10,8},{12,10},{14,12},{16,14},{18,... | collective-permute-start | bytes 393224 | tf_op jit(solution)/shard_map/ppermute | solution.py:17
  295.9 5.7 %collective-permute-start.57 = (bf16[4,128,128]{1,2,0:T(8,128)(2,1)S(1)}, bf16[4,128,128]{1,2,0:T(8,128)(2,1)S(1)}, u32[]{:S(2)}, u32[]{:S(2)}) collective-permute-start(bf16[4,128,128]{1,2,0:T(8,128)(2,1)S(1)} %collective-permute-done.56), channel_id=1, source_target_pairs={{0,30},{2,0},{4,2},{6,4},{8,6},{10,8},{12,10},{14,12},{16,14},{18,... | collective-permute-start | bytes 393224 | tf_op jit(solution)/shard_map/ppermute | solution.py:17
  305.1 5.6 %collective-permute-start.58 = (bf16[4,128,128]{1,2,0:T(8,128)(2,1)S(1)}, bf16[4,128,128]{1,2,0:T(8,128)(2,1)S(1)}, u32[]{:S(2)}, u32[]{:S(2)}) collective-permute-start(bf16[4,128,128]{1,2,0:T(8,128)(2,1)S(1)} %collective-permute-done.57), channel_id=1, source_target_pairs={{0,30},{2,0},{4,2},{6,4},{8,6},{10,8},{12,10},{14,12},{16,14},{18,... | collective-permute-start | bytes 393224 | tf_op jit(solution)/shard_map/ppermute | solution.py:17
  313.8 5.7 %collective-permute-start.59 = (bf16[4,128,128]{1,2,0:T(8,128)(2,1)S(1)}, bf16[4,128,128]{1,2,0:T(8,128)(2,1)S(1)}, u32[]{:S(2)}, u32[]{:S(2)}) collective-permute-start(bf16[4,128,128]{1,2,0:T(8,128)(2,1)S(1)} %collective-permute-done.58), channel_id=1, source_target_pairs={{0,30},{2,0},{4,2},{6,4},{8,6},{10,8},{12,10},{14,12},{16,14},{18,... | collective-permute-start | bytes 393224 | tf_op jit(solution)/shard_map/ppermute | solution.py:17
  333.3 9.9 %collective-permute-done.60 = bf16[4,128,128]{1,2,0:T(8,128)(2,1)S(1)} collective-permute-done((bf16[4,128,128]{1,2,0:T(8,128)(2,1)S(1)}, bf16[4,128,128]{1,2,0:T(8,128)(2,1)S(1)}, u32[]{:S(2)}, u32[]{:S(2)}) %collective-permute-start.60) | collective-permute-done | bytes 131104 | tf_op jit(solution)/shard_map/ppermute | solution.py:15
  343.2 5.6 %collective-permute-start.68 = (bf16[4,128,128]{1,2,0:T(8,128)(2,1)S(1)}, bf16[4,128,128]{1,2,0:T(8,128)(2,1)S(1)}, u32[]{:S(2)}, u32[]{:S(2)}) collective-permute-start(bf16[4,128,128]{1,2,0:T(8,128)(2,1)S(1)} %fusion.16), channel_id=1, source_target_pairs={{0,30},{2,0},{4,2},{6,4},{8,6},{10,8},{12,10},{14,12},{16,14},{18,... | collective-permute-start | bytes 393224 | tf_op jit(solution)/shard_map/ppermute | solution.py:17
  348.8 3.6 collective-permute-done.61
  352.4 5.6 %collective-permute-start.69 = (bf16[4,128,128]{1,2,0:T(8,128)(2,1)S(1)}, bf16[4,128,128]{1,2,0:T(8,128)(2,1)S(1)}, u32[]{:S(2)}, u32[]{:S(2)}) collective-permute-start(bf16[4,128,128]{1,2,0:T(8,128)(2,1)S(1)} %collective-permute-done.68), channel_id=1, source_target_pairs={{0,30},{2,0},{4,2},{6,4},{8,6},{10,8},{12,10},{14,12},{16,14},{18,... | collective-permute-start | bytes 393224 | tf_op jit(solution)/shard_map/ppermute | solution.py:17
  361.0 5.7 %collective-permute-start.70 = (bf16[4,128,128]{1,2,0:T(8,128)(2,1)S(1)}, bf16[4,128,128]{1,2,0:T(8,128)(2,1)S(1)}, u32[]{:S(2)}, u32[]{:S(2)}) collective-permute-start(bf16[4,128,128]{1,2,0:T(8,128)(2,1)S(1)} %collective-permute-done.69), channel_id=1, source_target_pairs={{0,30},{2,0},{4,2},{6,4},{8,6},{10,8},{12,10},{14,12},{16,14},{18,... | collective-permute-start | bytes 393224 | tf_op jit(solution)/shard_map/ppermute | solution.py:17
  369.6 5.7 %collective-permute-start.71 = (bf16[4,128,128]{1,2,0:T(8,128)(2,1)S(1)}, bf16[4,128,128]{1,2,0:T(8,128)(2,1)S(1)}, u32[]{:S(2)}, u32[]{:S(2)}) collective-permute-start(bf16[4,128,128]{1,2,0:T(8,128)(2,1)S(1)} %collective-permute-done.70), channel_id=1, source_target_pairs={{0,30},{2,0},{4,2},{6,4},{8,6},{10,8},{12,10},{14,12},{16,14},{18,... | collective-permute-start | bytes 393224 | tf_op jit(solution)/shard_map/ppermute | solution.py:17
  378.2 5.7 %collective-permute-start.72 = (bf16[4,128,128]{1,2,0:T(8,128)(2,1)S(1)}, bf16[4,128,128]{1,2,0:T(8,128)(2,1)S(1)}, u32[]{:S(2)}, u32[]{:S(2)}) collective-permute-start(bf16[4,128,128]{1,2,0:T(8,128)(2,1)S(1)} %collective-permute-done.71), channel_id=1, source_target_pairs={{0,30},{2,0},{4,2},{6,4},{8,6},{10,8},{12,10},{14,12},{16,14},{18,... | collective-permute-start | bytes 393224 | tf_op jit(solution)/shard_map/ppermute | solution.py:17
  386.7 5.7 %collective-permute-start.73 = (bf16[4,128,128]{1,2,0:T(8,128)(2,1)S(1)}, bf16[4,128,128]{1,2,0:T(8,128)(2,1)S(1)}, u32[]{:S(2)}, u32[]{:S(2)}) collective-permute-start(bf16[4,128,128]{1,2,0:T(8,128)(2,1)S(1)} %collective-permute-done.72), channel_id=1, source_target_pairs={{0,30},{2,0},{4,2},{6,4},{8,6},{10,8},{12,10},{14,12},{16,14},{18,... | collective-permute-start | bytes 393224 | tf_op jit(solution)/shard_map/ppermute | solution.py:17
  395.4 5.7 %collective-permute-start.74 = (bf16[4,128,128]{1,2,0:T(8,128)(2,1)S(1)}, bf16[4,128,128]{1,2,0:T(8,128)(2,1)S(1)}, u32[]{:S(2)}, u32[]{:S(2)}) collective-permute-start(bf16[4,128,128]{1,2,0:T(8,128)(2,1)S(1)} %collective-permute-done.73), channel_id=1, source_target_pairs={{0,30},{2,0},{4,2},{6,4},{8,6},{10,8},{12,10},{14,12},{16,14},{18,... | collective-permute-start | bytes 393224 | tf_op jit(solution)/shard_map/ppermute | solution.py:17
  (229 shorter events, 130.9 us)
Async XLA Ops:
  0.0 10.7 %collective-permute-start = (bf16[4,128,128]{2,1,0:T(8,128)(2,1)}, bf16[4,128,128]{2,1,0:T(8,128)(2,1)S(1)}, u32[]{:S(2)}, u32[]{:S(2)}) collective-permute-start(bf16[4,128,128]{2,1,0:T(8,128)(2,1)} %bitcast.45), channel_id=1, source_target_pairs={{0,2},{2,4},{4,6},{6,8},{8,10},{10,12},{12,14},{14,16},{16,18},{18... | collective-permute-start | bytes 393224 | tf_op jit(solution)/shard_map/ppermute | solution.py:15
  10.7 8.7 %collective-permute-start.1 = (bf16[4,128,128]{2,1,0:T(8,128)(2,1)S(1)}, bf16[4,128,128]{2,1,0:T(8,128)(2,1)S(1)}, u32[]{:S(2)}, u32[]{:S(2)}) collective-permute-start(bf16[4,128,128]{2,1,0:T(8,128)(2,1)S(1)} %collective-permute-done), channel_id=1, source_target_pairs={{0,2},{2,4},{4,6},{6,8},{8,10},{10,12},{12,14},{14,16},{16,18},{18... | collective-permute-start | bytes 393224 | tf_op jit(solution)/shard_map/ppermute | solution.py:15
  10.7 8.7 %collective-permute-start.8 = (bf16[4,128,128]{2,1,0:T(8,128)(2,1)}, bf16[4,128,128]{2,1,0:T(8,128)(2,1)S(1)}, u32[]{:S(2)}, u32[]{:S(2)}) collective-permute-start(bf16[4,128,128]{2,1,0:T(8,128)(2,1)} %bitcast.46), channel_id=1, source_target_pairs={{0,30},{2,0},{4,2},{6,4},{8,6},{10,8},{12,10},{14,12},{16,14},{18,... | collective-permute-start | bytes 393224 | tf_op jit(solution)/shard_map/ppermute | solution.py:17
  27.9 8.7 %collective-permute-start.3 = (bf16[4,128,128]{2,1,0:T(8,128)(2,1)S(1)}, bf16[4,128,128]{2,1,0:T(8,128)(2,1)S(1)}, u32[]{:S(2)}, u32[]{:S(2)}) collective-permute-start(bf16[4,128,128]{2,1,0:T(8,128)(2,1)S(1)} %collective-permute-done.2), channel_id=1, source_target_pairs={{0,2},{2,4},{4,6},{6,8},{8,10},{10,12},{12,14},{14,16},{16,18},{18... | collective-permute-start | bytes 393224 | tf_op jit(solution)/shard_map/ppermute | solution.py:15
  27.9 8.7 %collective-permute-start.10 = (bf16[4,128,128]{2,1,0:T(8,128)(2,1)S(1)}, bf16[4,128,128]{2,1,0:T(8,128)(2,1)S(1)}, u32[]{:S(2)}, u32[]{:S(2)}) collective-permute-start(bf16[4,128,128]{2,1,0:T(8,128)(2,1)S(1)} %collective-permute-done.9), channel_id=1, source_target_pairs={{0,30},{2,0},{4,2},{6,4},{8,6},{10,8},{12,10},{14,12},{16,14},{18,... | collective-permute-start | bytes 393224 | tf_op jit(solution)/shard_map/ppermute | solution.py:17
  36.6 8.7 %collective-permute-start.4 = (bf16[4,128,128]{2,1,0:T(8,128)(2,1)S(1)}, bf16[4,128,128]{2,1,0:T(8,128)(2,1)S(1)}, u32[]{:S(2)}, u32[]{:S(2)}) collective-permute-start(bf16[4,128,128]{2,1,0:T(8,128)(2,1)S(1)} %collective-permute-done.3), channel_id=1, source_target_pairs={{0,2},{2,4},{4,6},{6,8},{8,10},{10,12},{12,14},{14,16},{16,18},{18... | collective-permute-start | bytes 393224 | tf_op jit(solution)/shard_map/ppermute | solution.py:15
  36.6 9.4 %collective-permute-start.11 = (bf16[4,128,128]{2,1,0:T(8,128)(2,1)S(1)}, bf16[4,128,128]{2,1,0:T(8,128)(2,1)S(1)}, u32[]{:S(2)}, u32[]{:S(2)}) collective-permute-start(bf16[4,128,128]{2,1,0:T(8,128)(2,1)S(1)} %collective-permute-done.10), channel_id=1, source_target_pairs={{0,30},{2,0},{4,2},{6,4},{8,6},{10,8},{12,10},{14,12},{16,14},{18,... | collective-permute-start | bytes 393224 | tf_op jit(solution)/shard_map/ppermute | solution.py:17
  45.3 8.9 %collective-permute-start.5 = (bf16[4,128,128]{2,1,0:T(8,128)(2,1)S(1)}, bf16[4,128,128]{2,1,0:T(8,128)(2,1)S(1)}, u32[]{:S(2)}, u32[]{:S(2)}) collective-permute-start(bf16[4,128,128]{2,1,0:T(8,128)(2,1)S(1)} %collective-permute-done.4), channel_id=1, source_target_pairs={{0,2},{2,4},{4,6},{6,8},{8,10},{10,12},{12,14},{14,16},{16,18},{18... | collective-permute-start | bytes 393224 | tf_op jit(solution)/shard_map/ppermute | solution.py:15
  46.1 8.7 %collective-permute-start.12 = (bf16[4,128,128]{2,1,0:T(8,128)(2,1)S(1)}, bf16[4,128,128]{2,1,0:T(8,128)(2,1)S(1)}, u32[]{:S(2)}, u32[]{:S(2)}) collective-permute-start(bf16[4,128,128]{2,1,0:T(8,128)(2,1)S(1)} %collective-permute-done.11), channel_id=1, source_target_pairs={{0,30},{2,0},{4,2},{6,4},{8,6},{10,8},{12,10},{14,12},{16,14},{18,... | collective-permute-start | bytes 393224 | tf_op jit(solution)/shard_map/ppermute | solution.py:17
  54.2 10.1 %collective-permute-start.6 = (bf16[4,128,128]{2,1,0:T(8,128)(2,1)S(1)}, bf16[4,128,128]{2,1,0:T(8,128)(2,1)S(1)}, u32[]{:S(2)}, u32[]{:S(2)}) collective-permute-start(bf16[4,128,128]{2,1,0:T(8,128)(2,1)S(1)} %collective-permute-done.5), channel_id=1, source_target_pairs={{0,2},{2,4},{4,6},{6,8},{8,10},{10,12},{12,14},{14,16},{16,18},{18... | collective-permute-start | bytes 393224 | tf_op jit(solution)/shard_map/ppermute | solution.py:15
  54.7 11.9 %collective-permute-start.13 = (bf16[4,128,128]{2,1,0:T(8,128)(2,1)S(1)}, bf16[4,128,128]{2,1,0:T(8,128)(2,1)S(1)}, u32[]{:S(2)}, u32[]{:S(2)}) collective-permute-start(bf16[4,128,128]{2,1,0:T(8,128)(2,1)S(1)} %collective-permute-done.12), channel_id=1, source_target_pairs={{0,30},{2,0},{4,2},{6,4},{8,6},{10,8},{12,10},{14,12},{16,14},{18,... | collective-permute-start | bytes 393224 | tf_op jit(solution)/shard_map/ppermute | solution.py:17
  85.4 9.0 %collective-permute-start.15 = (bf16[4,128,128]{1,2,0:T(8,128)(2,1)S(1)}, bf16[4,128,128]{1,2,0:T(8,128)(2,1)S(1)}, u32[]{:S(2)}, u32[]{:S(2)}) collective-permute-start(bf16[4,128,128]{1,2,0:T(8,128)(2,1)S(1)} %fusion.7), channel_id=1, source_target_pairs={{0,2},{2,4},{4,6},{6,8},{8,10},{10,12},{12,14},{14,16},{16,18},{18... | collective-permute-start | bytes 393224 | tf_op jit(solution)/shard_map/ppermute | solution.py:15
  94.4 8.7 %collective-permute-start.16 = (bf16[4,128,128]{1,2,0:T(8,128)(2,1)S(1)}, bf16[4,128,128]{1,2,0:T(8,128)(2,1)S(1)}, u32[]{:S(2)}, u32[]{:S(2)}) collective-permute-start(bf16[4,128,128]{1,2,0:T(8,128)(2,1)S(1)} %collective-permute-done.15), channel_id=1, source_target_pairs={{0,2},{2,4},{4,6},{6,8},{8,10},{10,12},{12,14},{14,16},{16,18},{18... | collective-permute-start | bytes 393224 | tf_op jit(solution)/shard_map/ppermute | solution.py:15
  94.4 8.7 %collective-permute-start.23 = (bf16[4,128,128]{1,2,0:T(8,128)(2,1)S(1)}, bf16[4,128,128]{1,2,0:T(8,128)(2,1)S(1)}, u32[]{:S(2)}, u32[]{:S(2)}) collective-permute-start(bf16[4,128,128]{1,2,0:T(8,128)(2,1)S(1)} %fusion.7), channel_id=1, source_target_pairs={{0,30},{2,0},{4,2},{6,4},{8,6},{10,8},{12,10},{14,12},{16,14},{18,... | collective-permute-start | bytes 393224 | tf_op jit(solution)/shard_map/ppermute | solution.py:17
  103.1 8.7 %collective-permute-start.17 = (bf16[4,128,128]{1,2,0:T(8,128)(2,1)S(1)}, bf16[4,128,128]{1,2,0:T(8,128)(2,1)S(1)}, u32[]{:S(2)}, u32[]{:S(2)}) collective-permute-start(bf16[4,128,128]{1,2,0:T(8,128)(2,1)S(1)} %collective-permute-done.16), channel_id=1, source_target_pairs={{0,2},{2,4},{4,6},{6,8},{8,10},{10,12},{12,14},{14,16},{16,18},{18... | collective-permute-start | bytes 393224 | tf_op jit(solution)/shard_map/ppermute | solution.py:15
  103.1 8.7 %collective-permute-start.24 = (bf16[4,128,128]{1,2,0:T(8,128)(2,1)S(1)}, bf16[4,128,128]{1,2,0:T(8,128)(2,1)S(1)}, u32[]{:S(2)}, u32[]{:S(2)}) collective-permute-start(bf16[4,128,128]{1,2,0:T(8,128)(2,1)S(1)} %collective-permute-done.23), channel_id=1, source_target_pairs={{0,30},{2,0},{4,2},{6,4},{8,6},{10,8},{12,10},{14,12},{16,14},{18,... | collective-permute-start | bytes 393224 | tf_op jit(solution)/shard_map/ppermute | solution.py:17
  111.8 9.7 %collective-permute-start.18 = (bf16[4,128,128]{1,2,0:T(8,128)(2,1)S(1)}, bf16[4,128,128]{1,2,0:T(8,128)(2,1)S(1)}, u32[]{:S(2)}, u32[]{:S(2)}) collective-permute-start(bf16[4,128,128]{1,2,0:T(8,128)(2,1)S(1)} %collective-permute-done.17), channel_id=1, source_target_pairs={{0,2},{2,4},{4,6},{6,8},{8,10},{10,12},{12,14},{14,16},{16,18},{18... | collective-permute-start | bytes 393224 | tf_op jit(solution)/shard_map/ppermute | solution.py:15
  111.8 9.7 %collective-permute-start.25 = (bf16[4,128,128]{1,2,0:T(8,128)(2,1)S(1)}, bf16[4,128,128]{1,2,0:T(8,128)(2,1)S(1)}, u32[]{:S(2)}, u32[]{:S(2)}) collective-permute-start(bf16[4,128,128]{1,2,0:T(8,128)(2,1)S(1)} %collective-permute-done.24), channel_id=1, source_target_pairs={{0,30},{2,0},{4,2},{6,4},{8,6},{10,8},{12,10},{14,12},{16,14},{18,... | collective-permute-start | bytes 393224 | tf_op jit(solution)/shard_map/ppermute | solution.py:17
  121.5 9.3 %collective-permute-start.19 = (bf16[4,128,128]{1,2,0:T(8,128)(2,1)S(1)}, bf16[4,128,128]{1,2,0:T(8,128)(2,1)S(1)}, u32[]{:S(2)}, u32[]{:S(2)}) collective-permute-start(bf16[4,128,128]{1,2,0:T(8,128)(2,1)S(1)} %collective-permute-done.18), channel_id=1, source_target_pairs={{0,2},{2,4},{4,6},{6,8},{8,10},{10,12},{12,14},{14,16},{16,18},{18... | collective-permute-start | bytes 393224 | tf_op jit(solution)/shard_map/ppermute | solution.py:15
  121.5 9.3 %collective-permute-start.26 = (bf16[4,128,128]{1,2,0:T(8,128)(2,1)S(1)}, bf16[4,128,128]{1,2,0:T(8,128)(2,1)S(1)}, u32[]{:S(2)}, u32[]{:S(2)}) collective-permute-start(bf16[4,128,128]{1,2,0:T(8,128)(2,1)S(1)} %collective-permute-done.25), channel_id=1, source_target_pairs={{0,30},{2,0},{4,2},{6,4},{8,6},{10,8},{12,10},{14,12},{16,14},{18,... | collective-permute-start | bytes 393224 | tf_op jit(solution)/shard_map/ppermute | solution.py:17
  148.0 9.4 %collective-permute-start.22 = (bf16[4,128,128]{1,2,0:T(8,128)(2,1)S(1)}, bf16[4,128,128]{1,2,0:T(8,128)(2,1)S(1)}, u32[]{:S(2)}, u32[]{:S(2)}) collective-permute-start(bf16[4,128,128]{1,2,0:T(8,128)(2,1)S(1)} %collective-permute-done.21), channel_id=1, source_target_pairs={{0,2},{2,4},{4,6},{6,8},{8,10},{10,12},{12,14},{14,16},{16,18},{18... | collective-permute-start | bytes 393224 | tf_op jit(solution)/shard_map/ppermute | solution.py:15
  148.0 9.8 %collective-permute-start.29 = (bf16[4,128,128]{1,2,0:T(8,128)(2,1)S(1)}, bf16[4,128,128]{1,2,0:T(8,128)(2,1)S(1)}, u32[]{:S(2)}, u32[]{:S(2)}) collective-permute-start(bf16[4,128,128]{1,2,0:T(8,128)(2,1)S(1)} %collective-permute-done.28), channel_id=1, source_target_pairs={{0,30},{2,0},{4,2},{6,4},{8,6},{10,8},{12,10},{14,12},{16,14},{18,... | collective-permute-start | bytes 393224 | tf_op jit(solution)/shard_map/ppermute | solution.py:17
  168.3 8.7 %collective-permute-start.30 = (bf16[4,128,128]{1,2,0:T(8,128)(2,1)S(1)}, bf16[4,128,128]{1,2,0:T(8,128)(2,1)S(1)}, u32[]{:S(2)}, u32[]{:S(2)}) collective-permute-start(bf16[4,128,128]{1,2,0:T(8,128)(2,1)S(1)} %fusion.8), channel_id=1, source_target_pairs={{0,2},{2,4},{4,6},{6,8},{8,10},{10,12},{12,14},{14,16},{16,18},{18... | collective-permute-start | bytes 393224 | tf_op jit(solution)/shard_map/ppermute | solution.py:15
  177.0 8.7 %collective-permute-start.31 = (bf16[4,128,128]{1,2,0:T(8,128)(2,1)S(1)}, bf16[4,128,128]{1,2,0:T(8,128)(2,1)S(1)}, u32[]{:S(2)}, u32[]{:S(2)}) collective-permute-start(bf16[4,128,128]{1,2,0:T(8,128)(2,1)S(1)} %collective-permute-done.30), channel_id=1, source_target_pairs={{0,2},{2,4},{4,6},{6,8},{8,10},{10,12},{12,14},{14,16},{16,18},{18... | collective-permute-start | bytes 393224 | tf_op jit(solution)/shard_map/ppermute | solution.py:15
  177.0 8.7 %collective-permute-start.38 = (bf16[4,128,128]{1,2,0:T(8,128)(2,1)S(1)}, bf16[4,128,128]{1,2,0:T(8,128)(2,1)S(1)}, u32[]{:S(2)}, u32[]{:S(2)}) collective-permute-start(bf16[4,128,128]{1,2,0:T(8,128)(2,1)S(1)} %fusion.8), channel_id=1, source_target_pairs={{0,30},{2,0},{4,2},{6,4},{8,6},{10,8},{12,10},{14,12},{16,14},{18,... | collective-permute-start | bytes 393224 | tf_op jit(solution)/shard_map/ppermute | solution.py:17
  185.7 9.8 %collective-permute-start.32 = (bf16[4,128,128]{1,2,0:T(8,128)(2,1)S(1)}, bf16[4,128,128]{1,2,0:T(8,128)(2,1)S(1)}, u32[]{:S(2)}, u32[]{:S(2)}) collective-permute-start(bf16[4,128,128]{1,2,0:T(8,128)(2,1)S(1)} %collective-permute-done.31), channel_id=1, source_target_pairs={{0,2},{2,4},{4,6},{6,8},{8,10},{10,12},{12,14},{14,16},{16,18},{18... | collective-permute-start | bytes 393224 | tf_op jit(solution)/shard_map/ppermute | solution.py:15
  185.7 9.8 %collective-permute-start.39 = (bf16[4,128,128]{1,2,0:T(8,128)(2,1)S(1)}, bf16[4,128,128]{1,2,0:T(8,128)(2,1)S(1)}, u32[]{:S(2)}, u32[]{:S(2)}) collective-permute-start(bf16[4,128,128]{1,2,0:T(8,128)(2,1)S(1)} %collective-permute-done.38), channel_id=1, source_target_pairs={{0,30},{2,0},{4,2},{6,4},{8,6},{10,8},{12,10},{14,12},{16,14},{18,... | collective-permute-start | bytes 393224 | tf_op jit(solution)/shard_map/ppermute | solution.py:17
  195.5 9.2 %collective-permute-start.33 = (bf16[4,128,128]{1,2,0:T(8,128)(2,1)S(1)}, bf16[4,128,128]{1,2,0:T(8,128)(2,1)S(1)}, u32[]{:S(2)}, u32[]{:S(2)}) collective-permute-start(bf16[4,128,128]{1,2,0:T(8,128)(2,1)S(1)} %collective-permute-done.32), channel_id=1, source_target_pairs={{0,2},{2,4},{4,6},{6,8},{8,10},{10,12},{12,14},{14,16},{16,18},{18... | collective-permute-start | bytes 393224 | tf_op jit(solution)/shard_map/ppermute | solution.py:15
  195.5 9.2 %collective-permute-start.40 = (bf16[4,128,128]{1,2,0:T(8,128)(2,1)S(1)}, bf16[4,128,128]{1,2,0:T(8,128)(2,1)S(1)}, u32[]{:S(2)}, u32[]{:S(2)}) collective-permute-start(bf16[4,128,128]{1,2,0:T(8,128)(2,1)S(1)} %collective-permute-done.39), channel_id=1, source_target_pairs={{0,30},{2,0},{4,2},{6,4},{8,6},{10,8},{12,10},{14,12},{16,14},{18,... | collective-permute-start | bytes 393224 | tf_op jit(solution)/shard_map/ppermute | solution.py:17
  204.7 8.7 %collective-permute-start.34 = (bf16[4,128,128]{1,2,0:T(8,128)(2,1)S(1)}, bf16[4,128,128]{1,2,0:T(8,128)(2,1)S(1)}, u32[]{:S(2)}, u32[]{:S(2)}) collective-permute-start(bf16[4,128,128]{1,2,0:T(8,128)(2,1)S(1)} %collective-permute-done.33), channel_id=1, source_target_pairs={{0,2},{2,4},{4,6},{6,8},{8,10},{10,12},{12,14},{14,16},{16,18},{18... | collective-permute-start | bytes 393224 | tf_op jit(solution)/shard_map/ppermute | solution.py:15
  204.7 8.7 %collective-permute-start.41 = (bf16[4,128,128]{1,2,0:T(8,128)(2,1)S(1)}, bf16[4,128,128]{1,2,0:T(8,128)(2,1)S(1)}, u32[]{:S(2)}, u32[]{:S(2)}) collective-permute-start(bf16[4,128,128]{1,2,0:T(8,128)(2,1)S(1)} %collective-permute-done.40), channel_id=1, source_target_pairs={{0,30},{2,0},{4,2},{6,4},{8,6},{10,8},{12,10},{14,12},{16,14},{18,... | collective-permute-start | bytes 393224 | tf_op jit(solution)/shard_map/ppermute | solution.py:17
  221.9 9.4 %collective-permute-start.36 = (bf16[4,128,128]{1,2,0:T(8,128)(2,1)S(1)}, bf16[4,128,128]{1,2,0:T(8,128)(2,1)S(1)}, u32[]{:S(2)}, u32[]{:S(2)}) collective-permute-start(bf16[4,128,128]{1,2,0:T(8,128)(2,1)S(1)} %collective-permute-done.35), channel_id=1, source_target_pairs={{0,2},{2,4},{4,6},{6,8},{8,10},{10,12},{12,14},{14,16},{16,18},{18... | collective-permute-start | bytes 393224 | tf_op jit(solution)/shard_map/ppermute | solution.py:15
  221.9 9.4 %collective-permute-start.43 = (bf16[4,128,128]{1,2,0:T(8,128)(2,1)S(1)}, bf16[4,128,128]{1,2,0:T(8,128)(2,1)S(1)}, u32[]{:S(2)}, u32[]{:S(2)}) collective-permute-start(bf16[4,128,128]{1,2,0:T(8,128)(2,1)S(1)} %collective-permute-done.42), channel_id=1, source_target_pairs={{0,30},{2,0},{4,2},{6,4},{8,6},{10,8},{12,10},{14,12},{16,14},{18,... | collective-permute-start | bytes 393224 | tf_op jit(solution)/shard_map/ppermute | solution.py:17
  231.3 9.0 %collective-permute-start.44 = (bf16[4,128,128]{1,2,0:T(8,128)(2,1)S(1)}, bf16[4,128,128]{1,2,0:T(8,128)(2,1)S(1)}, u32[]{:S(2)}, u32[]{:S(2)}) collective-permute-start(bf16[4,128,128]{1,2,0:T(8,128)(2,1)S(1)} %collective-permute-done.43), channel_id=1, source_target_pairs={{0,30},{2,0},{4,2},{6,4},{8,6},{10,8},{12,10},{14,12},{16,14},{18,... | collective-permute-start | bytes 393224 | tf_op jit(solution)/shard_map/ppermute | solution.py:17
  250.8 8.8 %collective-permute-start.45 = (bf16[4,128,128]{1,2,0:T(8,128)(2,1)S(1)}, bf16[4,128,128]{1,2,0:T(8,128)(2,1)S(1)}, u32[]{:S(2)}, u32[]{:S(2)}) collective-permute-start(bf16[4,128,128]{1,2,0:T(8,128)(2,1)S(1)} %fusion.12), channel_id=1, source_target_pairs={{0,2},{2,4},{4,6},{6,8},{8,10},{10,12},{12,14},{14,16},{16,18},{18... | collective-permute-start | bytes 393224 | tf_op jit(solution)/shard_map/ppermute | solution.py:15
  259.6 9.9 %collective-permute-start.46 = (bf16[4,128,128]{1,2,0:T(8,128)(2,1)S(1)}, bf16[4,128,128]{1,2,0:T(8,128)(2,1)S(1)}, u32[]{:S(2)}, u32[]{:S(2)}) collective-permute-start(bf16[4,128,128]{1,2,0:T(8,128)(2,1)S(1)} %collective-permute-done.45), channel_id=1, source_target_pairs={{0,2},{2,4},{4,6},{6,8},{8,10},{10,12},{12,14},{14,16},{16,18},{18... | collective-permute-start | bytes 393224 | tf_op jit(solution)/shard_map/ppermute | solution.py:15
  259.6 9.9 %collective-permute-start.53 = (bf16[4,128,128]{1,2,0:T(8,128)(2,1)S(1)}, bf16[4,128,128]{1,2,0:T(8,128)(2,1)S(1)}, u32[]{:S(2)}, u32[]{:S(2)}) collective-permute-start(bf16[4,128,128]{1,2,0:T(8,128)(2,1)S(1)} %fusion.12), channel_id=1, source_target_pairs={{0,30},{2,0},{4,2},{6,4},{8,6},{10,8},{12,10},{14,12},{16,14},{18,... | collective-permute-start | bytes 393224 | tf_op jit(solution)/shard_map/ppermute | solution.py:17
  269.5 9.1 %collective-permute-start.47 = (bf16[4,128,128]{1,2,0:T(8,128)(2,1)S(1)}, bf16[4,128,128]{1,2,0:T(8,128)(2,1)S(1)}, u32[]{:S(2)}, u32[]{:S(2)}) collective-permute-start(bf16[4,128,128]{1,2,0:T(8,128)(2,1)S(1)} %collective-permute-done.46), channel_id=1, source_target_pairs={{0,2},{2,4},{4,6},{6,8},{8,10},{10,12},{12,14},{14,16},{16,18},{18... | collective-permute-start | bytes 393224 | tf_op jit(solution)/shard_map/ppermute | solution.py:15
  269.5 9.1 %collective-permute-start.54 = (bf16[4,128,128]{1,2,0:T(8,128)(2,1)S(1)}, bf16[4,128,128]{1,2,0:T(8,128)(2,1)S(1)}, u32[]{:S(2)}, u32[]{:S(2)}) collective-permute-start(bf16[4,128,128]{1,2,0:T(8,128)(2,1)S(1)} %collective-permute-done.53), channel_id=1, source_target_pairs={{0,30},{2,0},{4,2},{6,4},{8,6},{10,8},{12,10},{14,12},{16,14},{18,... | collective-permute-start | bytes 393224 | tf_op jit(solution)/shard_map/ppermute | solution.py:17
  278.6 8.7 %collective-permute-start.48 = (bf16[4,128,128]{1,2,0:T(8,128)(2,1)S(1)}, bf16[4,128,128]{1,2,0:T(8,128)(2,1)S(1)}, u32[]{:S(2)}, u32[]{:S(2)}) collective-permute-start(bf16[4,128,128]{1,2,0:T(8,128)(2,1)S(1)} %collective-permute-done.47), channel_id=1, source_target_pairs={{0,2},{2,4},{4,6},{6,8},{8,10},{10,12},{12,14},{14,16},{16,18},{18... | collective-permute-start | bytes 393224 | tf_op jit(solution)/shard_map/ppermute | solution.py:15
  278.6 8.7 %collective-permute-start.55 = (bf16[4,128,128]{1,2,0:T(8,128)(2,1)S(1)}, bf16[4,128,128]{1,2,0:T(8,128)(2,1)S(1)}, u32[]{:S(2)}, u32[]{:S(2)}) collective-permute-start(bf16[4,128,128]{1,2,0:T(8,128)(2,1)S(1)} %collective-permute-done.54), channel_id=1, source_target_pairs={{0,30},{2,0},{4,2},{6,4},{8,6},{10,8},{12,10},{14,12},{16,14},{18,... | collective-permute-start | bytes 393224 | tf_op jit(solution)/shard_map/ppermute | solution.py:17
  295.8 9.3 %collective-permute-start.50 = (bf16[4,128,128]{1,2,0:T(8,128)(2,1)S(1)}, bf16[4,128,128]{1,2,0:T(8,128)(2,1)S(1)}, u32[]{:S(2)}, u32[]{:S(2)}) collective-permute-start(bf16[4,128,128]{1,2,0:T(8,128)(2,1)S(1)} %collective-permute-done.49), channel_id=1, source_target_pairs={{0,2},{2,4},{4,6},{6,8},{8,10},{10,12},{12,14},{14,16},{16,18},{18... | collective-permute-start | bytes 393224 | tf_op jit(solution)/shard_map/ppermute | solution.py:15
  295.9 9.3 %collective-permute-start.57 = (bf16[4,128,128]{1,2,0:T(8,128)(2,1)S(1)}, bf16[4,128,128]{1,2,0:T(8,128)(2,1)S(1)}, u32[]{:S(2)}, u32[]{:S(2)}) collective-permute-start(bf16[4,128,128]{1,2,0:T(8,128)(2,1)S(1)} %collective-permute-done.56), channel_id=1, source_target_pairs={{0,30},{2,0},{4,2},{6,4},{8,6},{10,8},{12,10},{14,12},{16,14},{18,... | collective-permute-start | bytes 393224 | tf_op jit(solution)/shard_map/ppermute | solution.py:17
  313.8 9.0 %collective-permute-start.59 = (bf16[4,128,128]{1,2,0:T(8,128)(2,1)S(1)}, bf16[4,128,128]{1,2,0:T(8,128)(2,1)S(1)}, u32[]{:S(2)}, u32[]{:S(2)}) collective-permute-start(bf16[4,128,128]{1,2,0:T(8,128)(2,1)S(1)} %collective-permute-done.58), channel_id=1, source_target_pairs={{0,30},{2,0},{4,2},{6,4},{8,6},{10,8},{12,10},{14,12},{16,14},{18,... | collective-permute-start | bytes 393224 | tf_op jit(solution)/shard_map/ppermute | solution.py:17
  333.2 10.0 %collective-permute-start.60 = (bf16[4,128,128]{1,2,0:T(8,128)(2,1)S(1)}, bf16[4,128,128]{1,2,0:T(8,128)(2,1)S(1)}, u32[]{:S(2)}, u32[]{:S(2)}) collective-permute-start(bf16[4,128,128]{1,2,0:T(8,128)(2,1)S(1)} %fusion.16), channel_id=1, source_target_pairs={{0,2},{2,4},{4,6},{6,8},{8,10},{10,12},{12,14},{14,16},{16,18},{18... | collective-permute-start | bytes 393224 | tf_op jit(solution)/shard_map/ppermute | solution.py:15
  343.2 9.2 %collective-permute-start.61 = (bf16[4,128,128]{1,2,0:T(8,128)(2,1)S(1)}, bf16[4,128,128]{1,2,0:T(8,128)(2,1)S(1)}, u32[]{:S(2)}, u32[]{:S(2)}) collective-permute-start(bf16[4,128,128]{1,2,0:T(8,128)(2,1)S(1)} %collective-permute-done.60), channel_id=1, source_target_pairs={{0,2},{2,4},{4,6},{6,8},{8,10},{10,12},{12,14},{14,16},{16,18},{18... | collective-permute-start | bytes 393224 | tf_op jit(solution)/shard_map/ppermute | solution.py:15
  343.2 9.2 %collective-permute-start.68 = (bf16[4,128,128]{1,2,0:T(8,128)(2,1)S(1)}, bf16[4,128,128]{1,2,0:T(8,128)(2,1)S(1)}, u32[]{:S(2)}, u32[]{:S(2)}) collective-permute-start(bf16[4,128,128]{1,2,0:T(8,128)(2,1)S(1)} %fusion.16), channel_id=1, source_target_pairs={{0,30},{2,0},{4,2},{6,4},{8,6},{10,8},{12,10},{14,12},{16,14},{18,... | collective-permute-start | bytes 393224 | tf_op jit(solution)/shard_map/ppermute | solution.py:17
  395.4 8.9 %collective-permute-start.74 = (bf16[4,128,128]{1,2,0:T(8,128)(2,1)S(1)}, bf16[4,128,128]{1,2,0:T(8,128)(2,1)S(1)}, u32[]{:S(2)}, u32[]{:S(2)}) collective-permute-start(bf16[4,128,128]{1,2,0:T(8,128)(2,1)S(1)} %collective-permute-done.73), channel_id=1, source_target_pairs={{0,30},{2,0},{4,2},{6,4},{8,6},{10,8},{12,10},{14,12},{16,14},{18,... | collective-permute-start | bytes 393224 | tf_op jit(solution)/shard_map/ppermute | solution.py:17
  (34 other events, 369.6 us)
